TPU v7x, 512 devices: a whole 4x8x8 slice. The times are simulated.
512 devices in a mesh: row: 16 (over y, x_lo), col: 16 (over z, core), ka: 2 (over x_hi).
Axes of the slice: x: 4 (x_hi: 2, x_lo: 2; x = x_hi * 2 + x_lo), y: 8, z: 8, core: 2. Of those that a mesh axis runs over, the one named last changes fastest.
Arguments:
- pair: bfloat16 [512, 512, 128], P('row', ('col', 'ka')), may hold values from -6 to 6
- pair_mask: int32 [512, 512], P('row', ('col', 'ka')), may hold values from 0 to 1, as said below
- w_in: bfloat16 [2, 128, 512], replicated, may hold values from -0.5 to 0.5
- w_gate: bfloat16 [2, 128, 128], replicated, may hold values from -0.5 to 0.5
- w_out: bfloat16 [2, 128, 128], replicated, may hold values from -0.5 to 0.5
Outputs:
- updated: bfloat16 [512, 512, 128], P('row', ('col', 'ka'))
Inputs may be any that keep to these rules, and one draw needn't show every extreme that they name: pair_mask[i, j] = v[i] v[j] for a per-token 0/1 validity v; within each aligned run of 16 tokens the real tokens come first and there is at least one.
All inputs are finite; a program needn't handle non-finite values.
Results may differ from a plain program's by a relative error of at most 0.014.
Values may be sent and summed in bfloat16 or wider, within the bound.
No kernel may reach another device: no remote copies, remote signals or barrier semaphores. Data moves between devices by JAX's collectives and lax.ppermute only.
A program may use at most 64 MiB of HBM per device.

v0:
```python
import jax
import jax.numpy as jnp
from jax import lax
from jax.sharding import PartitionSpec as P


def from_root(value, axis, source):
    kept = jnp.where(lax.axis_index(axis) == source, value, 0).astype(value.dtype)
    return lax.psum(kept, axis)


def layer_norm(value):
    mean = jnp.mean(value, axis=-1, keepdims=True)
    centred = value - mean
    var = jnp.mean(centred * centred, axis=-1, keepdims=True)
    return centred / jnp.sqrt(var + 1e-05)


def prepare(pair, valid, weight_in, weight_gate):
    normed = layer_norm(pair.astype(jnp.float32)).astype(jnp.bfloat16)
    proj = jnp.einsum("ijc,cd->ijd", normed, weight_in, preferred_element_type=jnp.float32)
    width = proj.shape[-1] // 4
    left = (jax.nn.sigmoid(proj[..., :width]) * proj[..., width : 2 * width] * valid).astype(
        jnp.bfloat16
    )
    right = (
        jax.nn.sigmoid(proj[..., 2 * width : 3 * width]) * proj[..., 3 * width :] * valid
    ).astype(jnp.bfloat16)
    gate = jax.nn.sigmoid(
        jnp.einsum("ijc,cd->ijd", normed, weight_gate, preferred_element_type=jnp.float32)
    )
    return (left, right, gate)


def finish(pair, tri, gate, weight_out):
    normed = layer_norm(tri).astype(jnp.bfloat16)
    proj = jnp.einsum("ijc,cd->ijd", normed, weight_out, preferred_element_type=jnp.float32)
    return (pair.astype(jnp.float32) + gate * proj).astype(jnp.bfloat16)


def on_device(pair, pair_mask, w_in, w_gate, w_out):
    valid = pair_mask.astype(jnp.float32)[..., None]
    left, right, gate = prepare(pair, valid, w_in[0], w_gate[0])
    left_rows, right_rows = (
        lax.all_gather(left, "col", axis=1, tiled=True),
        lax.all_gather(right, "col", axis=1, tiled=True),
    )
    right_diag = from_root(right_rows, "row", lax.axis_index("col"))
    partial_value = jnp.einsum(
        "ikc,jkc->ijc", left_rows, right_diag, preferred_element_type=jnp.float32
    )
    tri = lax.psum_scatter(
        partial_value.astype(jnp.bfloat16), "ka", scatter_dimension=1, tiled=True
    ).astype(jnp.float32)
    middle = finish(pair, tri, gate, w_out[0])
    left, right, gate = prepare(middle, valid, w_in[1], w_gate[1])
    left_cols, right_cols = (
        lax.all_gather(left, "row", axis=0, tiled=True),
        lax.all_gather(right, "row", axis=0, tiled=True),
    )
    left_wide = lax.all_gather(left_cols, "ka", axis=1, tiled=True)
    left_diag = from_root(left_wide, "col", lax.axis_index("row"))
    tri = jnp.einsum("kic,kjc->ijc", left_diag, right_cols, preferred_element_type=jnp.float32)
    return finish(middle, tri, gate, w_out[1])


def solution(mesh):
    placed = (P("row", ("col", "ka"), None), P("row", ("col", "ka")), P(), P(), P())
    return jax.shard_map(
        on_device,
        mesh=mesh,
        in_specs=placed,
        out_specs=P("row", ("col", "ka"), None),
        check_vma=False,
    )
```

profile of v0, /device:TPU:1, one launch (start us, length us, event | category | flops | bytes accessed | tf_op | source)
XLA Modules:
  0.0 666.7 jit_solution(9475400611187420991)
XLA Ops:
  6.5 1.0 convert_reduce_fusion.1
  7.6 0.1 copy.43
  7.7 0.1 copy.44
  7.7 1.1 fusion.18
  8.9 0.1 copy.45
  9.0 0.1 copy.46
  9.1 0.7 convert_element_type.56
  9.8 0.1 copy.47
  9.8 1.3 fusion.42
  11.2 0.9 fusion.31
  12.0 0.0 all-gather.6.cloned.1.call-update
  12.1 0.0 all-gather.8.cloned.1.call-start
  12.1 0.7 all-gather.8.cloned.1.call-update
  12.8 0.0 all-reduce.3.cloned.1.call-start
  12.9 49.2 %all-gather.6.cloned.1.call-done = bf16[32,256,128]{2,1,0:T(8,128)(2,1)} async-done(((bf16[32,16,128]{2,1,0:T(8,128)(2,1)}), bf16[32,256,128]{2,1,0:T(8,128)(2,1)}) %all-gather.6.cloned.1.call-update) | async-done | bytes 2097168 | tf_op jit(solution)/shard_map/all_gather | solution.py:46
  62.0 1.4 broadcast_select_fusion.1
  63.5 0.0 all-reduce.3.cloned.1.call-update
  63.5 0.0 reduce-scatter.2.cloned.1.call-start
  63.6 43.2 %all-gather.8.cloned.1.call-done = bf16[32,256,128]{2,1,0:T(8,128)(2,1)} async-done(((bf16[32,16,128]{2,1,0:T(8,128)(2,1)}), bf16[32,256,128]{2,1,0:T(8,128)(2,1)}) %all-gather.8.cloned.1.call-update) | async-done | bytes 2097168 | tf_op jit(solution)/shard_map/all_gather | solution.py:45
  106.8 15.2 %copy.49 = bf16[32,256,128]{0,1,2:T(8,128)(2,1)} copy(bf16[32,256,128]{2,1,0:T(8,128)(2,1)} %all-gather.8.cloned.1.call-done) | data formatting | bytes 4194304 | tf_op jit(solution)/shard_map/all_gather | solution.py:45
  122.0 128.2 %all-reduce.3.cloned.1.call-done = bf16[32,256,128]{2,1,0:T(8,128)(2,1)} async-done(((bf16[32,256,128]{2,1,0:T(8,128)(2,1)}), bf16[32,256,128]{2,1,0:T(8,128)(2,1)}) %all-reduce.3.cloned.1.call-update) | async-done | bytes 2097168 | tf_op jit(solution)/shard_map/psum | solution.py:9
  250.2 3.4 copy.48
  253.6 0.0 copy-start
  253.6 0.0 copy-start.3
  253.6 5.8 fusion
  259.4 0.0 reduce-scatter.2.cloned.1.call-update
  259.5 0.0 copy-start.2
  259.5 0.0 all-gather.12.cloned.1.call-start
  259.5 0.0 copy-done
  259.6 0.3 fusion.10
  259.9 0.0 copy-start.1
  259.9 37.9 %reduce-scatter.2.cloned.1.call-done = bf16[32,16,128]{0,1,2:T(8,128)(2,1)} async-done(((bf16[32,32,128]{0,1,2:T(8,128)(2,1)}), bf16[32,16,128]{0,1,2:T(8,128)(2,1)}) %reduce-scatter.2.cloned.1.call-update) | async-done | bytes 131088 | tf_op jit(solution)/shard_map/reduce_scatter | solution.py:52
  297.8 1.2 convert_reduce_fusion
  299.0 1.3 fusion.14
  300.3 1.2 fusion.15
  301.5 0.5 copy.50
  302.0 0.3 fusion.56
  302.3 0.1 copy.51
  302.4 0.1 copy.52
  302.5 0.2 multiply_reduce_fusion.1
  302.7 0.1 copy.53
  302.8 0.1 copy.54
  302.9 0.4 fusion.40
  303.2 0.9 fusion.21
  304.1 0.0 all-gather.12.cloned.1.call-update
  304.1 0.0 all-gather.14.cloned.1.call-start
  304.2 64.7 %all-gather.12.cloned.1.call-done = bf16[512,16,128]{2,1,0:T(8,128)(2,1)} async-done(((bf16[32,16,128]{2,1,0:T(8,128)(2,1)}), bf16[512,16,128]{2,1,0:T(8,128)(2,1)}) %all-gather.12.cloned.1.call-update) | async-done | bytes 2097168 | tf_op jit(solution)/shard_map/all_gather | solution.py:58
  368.9 5.0 copy.55
  373.9 0.0 all-gather.14.cloned.1.call-update
  373.9 0.0 all-gather.10.cloned.1.call-start
  374.0 0.7 all-gather.10.cloned.1.call-update
  374.7 0.0 all-reduce.5.cloned.1.call-start
  374.7 74.4 %all-gather.14.cloned.1.call-done = bf16[512,32,128]{0,1,2:T(8,128)(2,1)} async-done(((bf16[512,16,128]{0,1,2:T(8,128)(2,1)}), bf16[512,32,128]{0,1,2:T(8,128)(2,1)}) %all-gather.14.cloned.1.call-update) | async-done | bytes 4194320 | tf_op jit(solution)/shard_map/all_gather | solution.py:61
  449.1 2.2 broadcast_select_fusion
  451.3 0.0 all-reduce.5.cloned.1.call-update
  451.3 0.3 fusion.7
  451.7 64.2 %all-gather.10.cloned.1.call-done = bf16[512,16,128]{2,1,0:T(8,128)(2,1)} async-done(((bf16[32,16,128]{2,1,0:T(8,128)(2,1)}), bf16[512,16,128]{2,1,0:T(8,128)(2,1)}) %all-gather.10.cloned.1.call-update) | async-done | bytes 2097168 | tf_op jit(solution)/shard_map/all_gather | solution.py:59
  515.8 3.9 copy.56
  519.8 135.0 %all-reduce.5.cloned.1.call-done = bf16[512,32,128]{0,1,2:T(8,128)(2,1)} async-done(((bf16[512,32,128]{0,1,2:T(8,128)(2,1)}), bf16[512,32,128]{0,1,2:T(8,128)(2,1)}) %all-reduce.5.cloned.1.call-update) | async-done | bytes 4194320 | tf_op jit(solution)/shard_map/psum | solution.py:9
  654.8 3.4 fusion.57
  658.2 0.2 multiply_reduce_fusion
  658.4 0.1 divide_convert_fusion
  658.5 0.5 copy.57
  659.0 0.8 fusion.13
  (12 shorter events, 0.1 us)
Async XLA Ops:
  6.5 55.5 %all-gather.6.cloned.1.call-start = ((), (), s32[]{:S(2)}) async-start(), calls=%async_computation.1 | async-start | bytes 2228224 | tf_op jit(solution)/shard_map/all_gather | solution.py:46
  12.1 94.7 %all-gather.8.cloned.1.call-start = ((), (), s32[]{:S(2)}) async-start(), calls=%async_computation.3 | async-start | bytes 2228224 | tf_op jit(solution)/shard_map/all_gather | solution.py:45
  12.8 237.4 %all-reduce.3.cloned.1.call-start = ((), (), s32[]{:S(2)}) async-start(), calls=%async_computation.2 | async-start | bytes 4194304 | tf_op jit(solution)/shard_map/psum | solution.py:9
  63.5 234.3 %reduce-scatter.2.cloned.1.call-start = ((), (), s32[]{:S(2)}) async-start(), calls=%async_computation.4 | async-start | bytes 1572864 | tf_op jit(solution)/shard_map/reduce_scatter | solution.py:52
  253.6 5.9 copy-start
  253.6 5.9 copy-start.3
  259.5 42.5 %copy-start.2 = (bf16[2,128,128]{2,1,0:T(8,128)(2,1)S(1)}, bf16[2,128,128]{2,1,0:T(8,128)(2,1)}, u32[]{:S(2)}) copy-start(bf16[2,128,128]{2,1,0:T(8,128)(2,1)} %param.9) | copy-start | bytes 196612
  259.5 109.4 %all-gather.12.cloned.1.call-start = ((), (), s32[]{:S(2)}) async-start(), calls=%async_computation.6 | async-start | bytes 2228224 | tf_op jit(solution)/shard_map/all_gather | solution.py:58
  259.9 43.0 %copy-start.1 = (bf16[2,128,512]{2,1,0:T(8,128)(2,1)S(1)}, bf16[2,128,512]{2,1,0:T(8,128)(2,1)}, u32[]{:S(2)}) copy-start(bf16[2,128,512]{2,1,0:T(8,128)(2,1)} %param.7) | copy-start | bytes 786436
  304.1 145.0 %all-gather.14.cloned.1.call-start = ((), (), s32[]{:S(2)}) async-start(), calls=%async_computation.7 | async-start | bytes 6291456 | tf_op jit(solution)/shard_map/all_gather | solution.py:61
  373.9 141.9 %all-gather.10.cloned.1.call-start = ((), (), s32[]{:S(2)}) async-start(), calls=%async_computation.5 | async-start | bytes 2228224 | tf_op jit(solution)/shard_map/all_gather | solution.py:59
  374.7 280.1 %all-reduce.5.cloned.1.call-start = ((), (), s32[]{:S(2)}) async-start(), calls=%async_computation.8 | async-start | bytes 8388608 | tf_op jit(solution)/shard_map/psum | solution.py:9
Sparse Core Ops, SparseCore 0:
  12.2 49.8 all-gather.5
  64.1 42.6 all-gather.7
  109.7 140.4 all-reduce.2
  259.6 38.2 reduce-scatter.1
  304.2 64.6 all-gather.11
  374.0 75.0 all-gather.13
  451.2 64.6 all-gather.9
  518.2 136.5 all-reduce.4
where the time goes:
time: 667 us
  waiting for transfers between devices  598 us (90%)
  local copies, waits for them, and re-layouts  29.2 us (4%)
  between operations  13.7 us (2%)
  matrix products  12.7 us (2%)
  other arithmetic  12.5 us (2%)
    psum x2, waiting for transfers between devices, from_root(): return lax.psum(kept, axis)  263 us
    all_gather x1, waiting for transfers between devices, on_device(): left_wide = lax.all_gather(left_cols, 'ka', axis=1, tiled=True)  74.4 us
    all_gather x1, waiting for transfers between devices, on_device(): lax.all_gather(left, 'row', axis=0, tiled=True)  64.7 us
    all_gather x1, waiting for transfers between devices, on_device(): lax.all_gather(right, 'row', axis=0, tiled=True)  64.2 us
    all_gather x1, waiting for transfers between devices, on_device(): lax.all_gather(right, 'col', axis=1, tiled=True)  49.2 us
    all_gather x1, waiting for transfers between devices, on_device(): lax.all_gather(left, 'col', axis=1, tiled=True)  43.2 us
    reduce_scatter x1, waiting for transfers between devices, on_device(): lax.psum_scatter(partial_value.astype(jnp.bfloat16), 'ka', scatter_dimens...  37.9 us
    all_gather x1, local copies, waits for them, and re-layouts, on_device(): lax.all_gather(left, 'col', axis=1, tiled=True)  15.2 us
  transfers between devices with their start and end apart: 8, of which 8 were waited for; matrix products, arithmetic and copies ran while one was open for 4% of the time, Pallas kernels for 0%

commit v1 on v0

--- a/solution.py
+++ b/solution.py
@@ -2,6 +2,28 @@
 import jax.numpy as jnp
 from jax import lax
 from jax.sharding import PartitionSpec as P
+
+
+def in_order(parts, dim):
+    shape = list(parts.shape[1:])
+    shape[dim] *= parts.shape[0]
+    return jnp.moveaxis(parts, 0, dim).reshape(shape)
+
+
+def gather_around(x, axis, dim):
+    length = lax.axis_size(axis)
+    pairs = [(i, (i + 1) % length) for i in range(length)]
+    back = [(b, a) for a, b in pairs]
+    lower, upper = ([], [])
+    for lap in range(length - 1):
+        if lap % 2 == 0:
+            lower.append(lax.ppermute(lower[-1] if lower else x, axis, pairs))
+        else:
+            upper.append(lax.ppermute(upper[-1] if upper else x, axis, back))
+    blocks = jnp.stack([*lower[::-1], x, *upper])
+    shift = lax.axis_index(axis) - len(lower)
+    blocks = blocks[(jnp.arange(length) - shift) % length]
+    return in_order(blocks, dim)
 
 
 def from_root(value, axis, source):
@@ -43,7 +65,7 @@
     left, right, gate = prepare(pair, valid, w_in[0], w_gate[0])
     left_rows, right_rows = (
         lax.all_gather(left, "col", axis=1, tiled=True),
-        lax.all_gather(right, "col", axis=1, tiled=True),
+        gather_around(right, "col", 1),
     )
     right_diag = from_root(right_rows, "row", lax.axis_index("col"))
     partial_value = jnp.einsum(

time: 667 us -> 564 us (0.85)
  waiting for transfers between devices: 598 us -> 444 us
  starting transfers between devices: 0.29 us -> 36.5 us
  local copies, waits for them, and re-layouts: 29.2 us -> 42.4 us
    psum x2, waiting for transfers between devices: 263 us -> 172 us  [from_root(): return lax.psum(kept, axis)]
    all_gather x1 -> x0, waiting for transfers between devices: 49.2 us -> none  [on_device(): lax.all_gather(right, 'col', axis=1, tiled=True)]
    ppermute x0 -> x15, starting transfers between devices: none -> 36.2 us  [the longest x7 32.5 us: gather_around(): upper.append(lax.ppermute(upper[-1] if upper else x, axis, back))]
    all_gather x1, waiting for transfers between devices: 43.2 us -> 20 us  [on_device(): lax.all_gather(left, 'col', axis=1, tiled=True)]
    ppermute x0 -> x15, waiting for transfers between devices: none -> 10.8 us  [the longest x8 9.89 us: gather_around(): lower.append(lax.ppermute(lower[-1] if lower else x, axis, pairs))]
    unnamed x8 -> x23, local copies, waits for them, and re-layouts: 0.03 us -> 9.86 us
  transfers between devices with their start and end apart: 8 -> 22, of which waited for: 8 -> 21; matrix products, arithmetic and copies ran while one was open for 4% -> 7% of each run, Pallas kernels for 0% -> 0%
where the time goes in v1:
time: 564 us; the launch traced here: 563 us
  waiting for transfers between devices  444 us (79%)
  local copies, waits for them, and re-layouts  42.4 us (8%)
  starting transfers between devices  36.5 us (6%)
  between operations  15.3 us (3%)
  matrix products  13.2 us (2%)
  other arithmetic  11.3 us (2%)
    psum x2, waiting for transfers between devices, from_root(): return lax.psum(kept, axis)  172 us
    all_gather x1, waiting for transfers between devices, on_device(): left_wide = lax.all_gather(left_cols, 'ka', axis=1, tiled=True)  74.2 us
    all_gather x1, waiting for transfers between devices, on_device(): lax.all_gather(left, 'row', axis=0, tiled=True)  64.4 us
    all_gather x1, waiting for transfers between devices, on_device(): lax.all_gather(right, 'row', axis=0, tiled=True)  64.4 us
    reduce_scatter x1, waiting for transfers between devices, on_device(): lax.psum_scatter(partial_value.astype(jnp.bfloat16), 'ka', scatter_dimens...  37.8 us
    ppermute x7, starting transfers between devices, gather_around(): upper.append(lax.ppermute(upper[-1] if upper else x, axis, back))  32.5 us
    all_gather x1, waiting for transfers between devices, on_device(): lax.all_gather(left, 'col', axis=1, tiled=True)  20 us
    all_gather x1, local copies, waits for them, and re-layouts, on_device(): lax.all_gather(left, 'col', axis=1, tiled=True)  15.2 us
  transfers between devices with their start and end apart: 22, of which 21 were waited for; matrix products, arithmetic and copies ran while one was open for 7% of the time, Pallas kernels for 0%

profile of v1, /device:TPU:1, one launch (start us, length us, event | category | flops | bytes accessed | tf_op | source)
XLA Modules:
  0.0 563.0 jit_solution(11387668872643815256)
XLA Ops:
  7.4 1.0 convert_reduce_fusion.1
  8.6 1.1 fusion.18
  9.9 0.7 convert_element_type.56
  10.7 1.3 fusion.42
  12.0 0.8 fusion.31
  12.8 3.5 collective-permute-start
  16.3 4.2 collective-permute-done
  20.7 4.8 collective-permute-start.8
  25.5 0.8 collective-permute-done.1
  26.4 4.6 collective-permute-start.9
  31.1 0.8 collective-permute-done.2
  32.0 4.6 collective-permute-start.10
  36.7 0.8 collective-permute-done.3
  37.7 4.6 collective-permute-start.11
  42.3 0.8 collective-permute-done.4
  43.3 4.6 collective-permute-start.12
  47.9 0.8 collective-permute-done.5
  48.9 4.7 collective-permute-start.13
  53.6 0.7 collective-permute-done.6
  54.6 4.6 collective-permute-start.14
  59.1 0.8 collective-permute-done.7
  59.9 0.6 bitcast_dynamic-update-slice_fusion.15
  60.6 0.7 bitcast_dynamic-update-slice_fusion.14
  61.2 0.7 bitcast_dynamic-update-slice_fusion.13
  61.9 0.6 bitcast_dynamic-update-slice_fusion.12
  62.5 0.7 bitcast_dynamic-update-slice_fusion.11
  63.2 0.7 bitcast_dynamic-update-slice_fusion.10
  63.8 0.7 bitcast_dynamic-update-slice_fusion.9
  64.5 0.7 bitcast_dynamic-update-slice_fusion.8
  65.2 0.6 bitcast_dynamic-update-slice_fusion.7
  65.8 0.7 bitcast_dynamic-update-slice_fusion.6
  66.5 0.7 bitcast_dynamic-update-slice_fusion.5
  67.1 0.7 bitcast_dynamic-update-slice_fusion.4
  67.8 0.7 bitcast_dynamic-update-slice_fusion.3
  68.4 0.7 bitcast_dynamic-update-slice_fusion.2
  69.1 0.7 bitcast_dynamic-update-slice_fusion.1
  69.8 0.7 bitcast_dynamic-update-slice_fusion
  70.4 2.5 gather_fusion
  73.1 0.6 copy.61
  73.7 3.0 copy.62
  76.8 20.0 %all-gather.5.cloned.1.call-done = bf16[32,256,128]{2,1,0:T(8,128)(2,1)} async-done(((bf16[32,16,128]{2,1,0:T(8,128)(2,1)}), bf16[32,256,128]{2,1,0:T(8,128)(2,1)}) %all-gather.5.cloned.1.call-update) | async-done | bytes 2097168 | tf_op jit(solution)/shard_map/all_gather | solution.py:67
  96.8 15.2 %copy.63 = bf16[32,256,128]{0,1,2:T(8,128)(2,1)} copy(bf16[32,256,128]{2,1,0:T(8,128)(2,1)} %all-gather.5.cloned.1.call-done) | data formatting | bytes 4194304 | tf_op jit(solution)/shard_map/all_gather | solution.py:67
  112.0 109.7 %all-reduce.3.cloned.1.call-done = bf16[32,256,128]{1,0,2:T(8,128)(2,1)} async-done(((bf16[32,256,128]{1,0,2:T(8,128)(2,1)}), bf16[32,256,128]{1,0,2:T(8,128)(2,1)}) %all-reduce.3.cloned.1.call-update) | async-done | bytes 2097168 | tf_op jit(solution)/shard_map/psum | solution.py:31
  221.7 6.4 %fusion = bf16[32,32,128]{0,1,2:T(8,128)(2,1)} fusion(bf16[32,256,128]{1,0,2:T(8,128)(2,1)} %all-reduce.3.cloned.1.call-done, bf16[32,256,128]{0,1,2:T(8,128)(2,1)} %copy.63), kind=kOutput, calls=%fused_computation.4 | convolution fusion | flops 67239936 | bytes 4456448 | tf_op jit(solution)/shard_map/ikc,jkc->ijc/dot_general | solution.py:71
  228.2 0.3 fusion.10
  228.6 37.8 %reduce-scatter.2.cloned.1.call-done = bf16[32,16,128]{0,1,2:T(8,128)(2,1)} async-done(((bf16[32,32,128]{0,1,2:T(8,128)(2,1)}), bf16[32,16,128]{0,1,2:T(8,128)(2,1)}) %reduce-scatter.2.cloned.1.call-update) | async-done | bytes 131088 | tf_op jit(solution)/shard_map/reduce_scatter | solution.py:74
  266.3 1.2 convert_reduce_fusion
  267.6 1.3 fusion.14
  268.8 1.2 fusion.15
  270.0 0.5 copy.64
  271.4 0.4 fusion.40
  271.7 0.9 fusion.21
  272.7 64.4 %all-gather.9.cloned.1.call-done = bf16[512,16,128]{2,1,0:T(8,128)(2,1)} async-done(((bf16[32,16,128]{2,1,0:T(8,128)(2,1)}), bf16[512,16,128]{2,1,0:T(8,128)(2,1)}) %all-gather.9.cloned.1.call-update) | async-done | bytes 2097168 | tf_op jit(solution)/shard_map/all_gather | solution.py:80
  337.1 4.9 copy.69
  342.1 0.7 all-gather.7.cloned.1.call-update
  342.9 74.2 %all-gather.11.cloned.1.call-done = bf16[512,32,128]{0,1,2:T(8,128)(2,1)} async-done(((bf16[512,16,128]{0,1,2:T(8,128)(2,1)}), bf16[512,32,128]{0,1,2:T(8,128)(2,1)}) %all-gather.11.cloned.1.call-update) | async-done | bytes 4194320 | tf_op jit(solution)/shard_map/all_gather | solution.py:83
  417.1 2.2 broadcast_select_fusion
  419.4 0.3 fusion.7
  419.7 64.4 %all-gather.7.cloned.1.call-done = bf16[512,16,128]{2,1,0:T(8,128)(2,1)} async-done(((bf16[32,16,128]{2,1,0:T(8,128)(2,1)}), bf16[512,16,128]{2,1,0:T(8,128)(2,1)}) %all-gather.7.cloned.1.call-update) | async-done | bytes 2097168 | tf_op jit(solution)/shard_map/all_gather | solution.py:81
  484.1 3.9 copy.70
  488.1 62.3 %all-reduce.5.cloned.1.call-done = bf16[512,32,128]{0,1,2:T(8,128)(2,1)} async-done(((bf16[512,32,128]{0,1,2:T(8,128)(2,1)}), bf16[512,32,128]{0,1,2:T(8,128)(2,1)}) %all-reduce.5.cloned.1.call-update) | async-done | bytes 4194320 | tf_op jit(solution)/shard_map/psum | solution.py:31
  550.3 3.4 fusion.59
  554.1 0.5 copy.71
  554.6 0.8 fusion.13
  (59 shorter events, 3.2 us)
Async XLA Ops:
  7.4 89.4 %all-gather.5.cloned.1.call-start = ((), (), s32[]{:S(2)}) async-start(), calls=%async_computation.2 | async-start | bytes 2228224 | tf_op jit(solution)/shard_map/all_gather | solution.py:67
  12.8 7.7 %collective-permute-start = (bf16[32,16,128]{2,1,0:T(8,128)(2,1)S(1)}, bf16[32,16,128]{2,1,0:T(8,128)(2,1)S(1)}, u32[]{:S(2)}, u32[]{:S(2)}) collective-permute-start(bf16[32,16,128]{2,1,0:T(8,128)(2,1)S(1)} %get-tuple-element.8), channel_id=1, source_target_pairs={{0,2},{2,4},{4,6},{6,8},{8,10},{10,12},{12,14},{14,16},{16,18},{18... | collective-permute-start | bytes 393224 | tf_op jit(solution)/shard_map/ppermute | solution.py:20
  20.5 5.8 %collective-permute-start.1 = (bf16[32,16,128]{2,1,0:T(8,128)(2,1)S(1)}, bf16[32,16,128]{2,1,0:T(8,128)(2,1)S(1)}, u32[]{:S(2)}, u32[]{:S(2)}) collective-permute-start(bf16[32,16,128]{2,1,0:T(8,128)(2,1)S(1)} %collective-permute-done), channel_id=1, source_target_pairs={{0,2},{2,4},{4,6},{6,8},{8,10},{10,12},{12,14},{14,16},{16,18},{18... | collective-permute-start | bytes 393224 | tf_op jit(solution)/shard_map/ppermute | solution.py:20
  20.7 5.7 %collective-permute-start.8 = (bf16[32,16,128]{2,1,0:T(8,128)(2,1)S(1)}, bf16[32,16,128]{2,1,0:T(8,128)(2,1)S(1)}, u32[]{:S(2)}, u32[]{:S(2)}) collective-permute-start(bf16[32,16,128]{2,1,0:T(8,128)(2,1)S(1)} %get-tuple-element.8), channel_id=1, source_target_pairs={{2,0},{4,2},{6,4},{8,6},{10,8},{12,10},{14,12},{16,14},{18,16},{20... | collective-permute-start | bytes 393224 | tf_op jit(solution)/shard_map/ppermute | solution.py:22
  26.3 5.6 collective-permute-start.2
  26.4 5.6 collective-permute-start.9
  31.9 5.6 collective-permute-start.3
  32.0 5.6 collective-permute-start.10
  37.5 5.6 collective-permute-start.4
  37.7 5.6 collective-permute-start.11
  43.1 5.6 collective-permute-start.5
  43.3 5.6 collective-permute-start.12
  48.7 5.6 collective-permute-start.6
  48.7 173.0 %all-reduce.3.cloned.1.call-start = ((), (), s32[]{:S(2)}) async-start(), calls=%async_computation.1 | async-start | bytes 4194304 | tf_op jit(solution)/shard_map/psum | solution.py:31
  48.9 5.7 %collective-permute-start.13 = (bf16[32,16,128]{2,1,0:T(8,128)(2,1)S(1)}, bf16[32,16,128]{2,1,0:T(8,128)(2,1)S(1)}, u32[]{:S(2)}, u32[]{:S(2)}) collective-permute-start(bf16[32,16,128]{2,1,0:T(8,128)(2,1)S(1)} %collective-permute-done.12), channel_id=1, source_target_pairs={{2,0},{4,2},{6,4},{8,6},{10,8},{12,10},{14,12},{16,14},{18,16},{20... | collective-permute-start | bytes 393224 | tf_op jit(solution)/shard_map/ppermute | solution.py:22
  54.3 5.6 collective-permute-start.7
  54.6 15.2 %collective-permute-start.14 = (bf16[32,16,128]{2,1,0:T(8,128)(2,1)S(1)}, bf16[32,16,128]{2,1,0:T(8,128)(2,1)S(1)}, u32[]{:S(2)}, u32[]{:S(2)}) collective-permute-start(bf16[32,16,128]{2,1,0:T(8,128)(2,1)S(1)} %collective-permute-done.13), channel_id=1, source_target_pairs={{2,0},{4,2},{6,4},{8,6},{10,8},{12,10},{14,12},{16,14},{18,16},{20... | collective-permute-start | bytes 393224 | tf_op jit(solution)/shard_map/ppermute | solution.py:22
  76.7 189.6 %reduce-scatter.2.cloned.1.call-start = ((), (), s32[]{:S(2)}) async-start(), calls=%async_computation.3 | async-start | bytes 1572864 | tf_op jit(solution)/shard_map/reduce_scatter | solution.py:74
  112.0 116.2 %copy-start = (bf16[32,16,128]{2,1,0:T(8,128)(2,1)S(1)}, bf16[32,16,128]{2,1,0:T(8,128)(2,1)}, u32[]{:S(2)}) copy-start(bf16[32,16,128]{2,1,0:T(8,128)(2,1)} %param.5) | copy-start | bytes 393220
  112.0 116.2 %copy-start.3 = (bf16[2,128,128]{2,1,0:T(8,128)(2,1)S(1)}, bf16[2,128,128]{2,1,0:T(8,128)(2,1)}, u32[]{:S(2)}) copy-start(bf16[2,128,128]{2,1,0:T(8,128)(2,1)} %param.8) | copy-start | bytes 196612
  228.1 42.4 %copy-start.2 = (bf16[2,128,128]{2,1,0:T(8,128)(2,1)S(1)}, bf16[2,128,128]{2,1,0:T(8,128)(2,1)}, u32[]{:S(2)}) copy-start(bf16[2,128,128]{2,1,0:T(8,128)(2,1)} %param.9) | copy-start | bytes 196612
  228.1 109.0 %all-gather.9.cloned.1.call-start = ((), (), s32[]{:S(2)}) async-start(), calls=%async_computation.5 | async-start | bytes 2228224 | tf_op jit(solution)/shard_map/all_gather | solution.py:80
  228.6 42.8 %copy-start.1 = (bf16[2,128,512]{2,1,0:T(8,128)(2,1)S(1)}, bf16[2,128,512]{2,1,0:T(8,128)(2,1)}, u32[]{:S(2)}) copy-start(bf16[2,128,512]{2,1,0:T(8,128)(2,1)} %param.7) | copy-start | bytes 786436
  272.6 144.5 %all-gather.11.cloned.1.call-start = ((), (), s32[]{:S(2)}) async-start(), calls=%async_computation.6 | async-start | bytes 6291456 | tf_op jit(solution)/shard_map/all_gather | solution.py:83
  342.1 142.1 %all-gather.7.cloned.1.call-start = ((), (), s32[]{:S(2)}) async-start(), calls=%async_computation.4 | async-start | bytes 2228224 | tf_op jit(solution)/shard_map/all_gather | solution.py:81
  342.8 207.5 %all-reduce.5.cloned.1.call-start = ((), (), s32[]{:S(2)}) async-start(), calls=%async_computation.7 | async-start | bytes 8388608 | tf_op jit(solution)/shard_map/psum | solution.py:31
Sparse Core Ops, SparseCore 0:
  48.9 47.8 all-gather.4
  419.5 130.8 all-reduce.4
Sparse Core Ops, SparseCore 1:
  76.8 144.8 all-reduce.2
  228.2 38.1 reduce-scatter.1
  272.7 64.3 all-gather.8
  342.1 74.9 all-gather.10
  419.2 64.9 all-gather.6
